TPU v7x, 32 devices: a whole 2x2x4 slice. The times are simulated.
32 devices in a mesh: dp: 2 (over y), seq: 16 (over z, x, core).
Axes of the slice: x: 2, y: 2, z: 4, core: 2. Of those that a mesh axis runs over, the one named last changes fastest.
Arguments:
- inputs: bfloat16 [2, 256, 512, 512], P('dp', 'seq'), may hold values from -6 to 6
- gate_logits: bfloat16 [2, 256, 512, 512], P('dp', 'seq'), may hold values from -8 to 8
- kernel: bfloat16 [256, 512, 512], P(None, 'seq'), may hold values from -1.5 to 1.5
- cotangent: bfloat16 [2, 256, 512, 512], P('dp', 'seq'), may hold values from -6 to 6
- block_one: bfloat16 [256, 512, 512], P('seq'), may hold values from -0.25 to 0.25
- block_two: bfloat16 [512, 256, 256], P('seq'), may hold values from -0.375 to 0.375
Outputs:
- output: bfloat16 [2, 256, 512, 512], P('dp', 'seq')
- grad_inputs: bfloat16 [2, 256, 512, 512], P('dp', 'seq')
- grad_gate: bfloat16 [2, 256, 512, 512], P('dp', 'seq')
- grad_kernel: bfloat16 [256, 512, 512], P(None, 'seq', 'dp')
- grad_block_one: bfloat16 [256, 512, 512], P('seq', None, 'dp')
- grad_block_two: bfloat16 [512, 256, 256], P('seq', None, 'dp')
All inputs are finite; a program needn't handle non-finite values.
Results may differ from a plain program's by a relative error of at most 0.009.
Values may be sent and summed in bfloat16 or wider, within the bound.
No kernel may reach another device: no remote copies, remote signals or barrier semaphores. Data moves between devices by JAX's collectives and lax.ppermute only.
A program may use at most 320 MiB of HBM per device.

v0:
```python
import jax
import jax.numpy as jnp
from jax import lax
from jax.sharding import PartitionSpec as P


def to_cols(x):
    return lax.all_to_all(x, "seq", split_axis=1, concat_axis=0, tiled=True)


def to_rows(x):
    return lax.all_to_all(x, "seq", split_axis=0, concat_axis=1, tiled=True)


def held(x):
    return lax.optimization_barrier(x)


def body(inputs, gate_logits, kernel, cotangent, block_one, block_two):
    tokens = inputs[0]
    kernel_wide = kernel.astype(jnp.float32)
    grad_scale = (lax.axis_size("dp") * tokens.shape[2]) ** (-0.5)
    f32 = jnp.float32
    opened = jax.nn.sigmoid(gate_logits[0].astype(f32))
    incoming = cotangent[0].astype(f32)
    grad_fourth = held((incoming * opened).astype(jnp.bfloat16))
    grad_third = jnp.einsum(
        "fch,fhd->fcd", block_one, grad_fourth, preferred_element_type=f32
    ).astype(jnp.bfloat16)
    grad_third_cols = to_cols(held(grad_third))
    first = jnp.einsum("acb,abd->acd", block_one, tokens, preferred_element_type=f32).astype(
        jnp.bfloat16
    )
    first, grad_third_cols = held((first, grad_third_cols))
    first_cols = to_cols(first)
    grad_filtered = held(
        jnp.einsum("cef,fcd->ecd", block_two, grad_third_cols, preferred_element_type=f32)
    )
    grad_second = (kernel_wide * grad_filtered).astype(jnp.bfloat16)
    grad_first = jnp.einsum(
        "cea,ecd->acd", block_two, grad_second, preferred_element_type=f32
    ).astype(jnp.bfloat16)
    grad_first, first_cols = held((grad_first, first_cols))
    grad_first_rows = to_rows(grad_first)
    second = held(jnp.einsum("cea,acd->ecd", block_two, first_cols, preferred_element_type=f32))
    filtered = (kernel_wide * second).astype(jnp.bfloat16)
    third = jnp.einsum("cef,ecd->fcd", block_two, filtered, preferred_element_type=f32).astype(
        jnp.bfloat16
    )
    third, grad_first_rows = held((third, grad_first_rows))
    third_rows = to_rows(third)
    grad_kernel = (grad_filtered * second).astype(jnp.bfloat16)
    grad_block_two = (
        (
            jnp.einsum("fcd,ecd->cef", grad_third_cols, filtered, preferred_element_type=f32)
            + jnp.einsum("ecd,acd->cea", grad_second, first_cols, preferred_element_type=f32)
        )
        * grad_scale
    ).astype(jnp.bfloat16)
    grad_kernel = lax.psum_scatter(grad_kernel, "dp", scatter_dimension=2, tiled=True)
    grad_block_two = lax.psum_scatter(grad_block_two, "dp", scatter_dimension=2, tiled=True)
    grad_tokens = jnp.einsum(
        "acb,acd->abd", block_one, grad_first_rows, preferred_element_type=f32
    ).astype(jnp.bfloat16)
    outer_inputs = jnp.einsum("acd,abd->acb", grad_first_rows, tokens, preferred_element_type=f32)
    fourth = jnp.einsum("fch,fcd->fhd", block_one, third_rows, preferred_element_type=f32).astype(
        jnp.bfloat16
    )
    fourth_wide = fourth.astype(f32)
    output = (opened * fourth_wide).astype(jnp.bfloat16)
    grad_gate = (incoming * fourth_wide * opened * (1.0 - opened)).astype(jnp.bfloat16)
    outer_one = jnp.einsum("fhd,fcd->fch", grad_fourth, third_rows, preferred_element_type=f32)
    grad_block_one = ((outer_one + outer_inputs) * grad_scale).astype(jnp.bfloat16)
    grad_block_one = lax.psum_scatter(grad_block_one, "dp", scatter_dimension=2, tiled=True)
    return (
        output[None],
        grad_tokens[None],
        grad_gate[None],
        grad_kernel,
        grad_block_one,
        grad_block_two,
    )


def solution(mesh):
    return jax.shard_map(
        body,
        mesh=mesh,
        in_specs=(
            P("dp", "seq", None, None),
            P("dp", "seq", None, None),
            P(None, "seq", None),
            P("dp", "seq", None, None),
            P("seq", None, None),
            P("seq", None, None),
        ),
        out_specs=(
            P("dp", "seq", None, None),
            P("dp", "seq", None, None),
            P("dp", "seq", None, None),
            P(None, "seq", "dp"),
            P("seq", None, "dp"),
            P("seq", None, "dp"),
        ),
        check_vma=False,
    )
```

profile of v0, /device:TPU:0, one launch (start us, length us, event | category | flops | bytes accessed | tf_op | source)
XLA Modules:
  0.0 1020.6 jit_solution(17853031852421777675)
XLA Ops:
  7.2 12.3 %copy.71 = bf16[1,16,512,512]{2,3,1,0:T(8,128)(2,1)} copy(bf16[1,16,512,512]{3,2,1,0:T(8,128)(2,1)} %param.7) | data formatting | bytes 16777216 | tf_op args[1]
  19.4 12.3 %copy.73 = bf16[1,16,512,512]{2,3,1,0:T(8,128)(2,1)} copy(bf16[1,16,512,512]{3,2,1,0:T(8,128)(2,1)} %param.9) | data formatting | bytes 16777216 | tf_op args[3]
  31.7 11.4 %fusion.2 = bf16[16,512,512]{1,2,0:T(8,128)(2,1)} fusion(bf16[1,16,512,512]{2,3,1,0:T(8,128)(2,1)} %copy.73, bf16[1,16,512,512]{2,3,1,0:T(8,128)(2,1)} %copy.71), kind=kLoop, calls=%fused_computation.6 | loop fusion | flops 29360128 | bytes 25165824 | tf_op jit(solution)/shard_map/convert_element_type | solution.py:26
  43.1 11.5 %convert_bitcast_fusion.3 = bf16[16,512,512]{1,2,0:T(8,128)(2,1)} fusion(bf16[16,512,512]{1,2,0:T(8,128)(2,1)} %fusion.2, bf16[16,512,512]{2,1,0:T(8,128)(2,1)} %param.10), kind=kOutput, calls=%fused_computation.28 | convolution fusion | flops 4299161600 | bytes 25165824 | tf_op jit(solution)/shard_map/fch,fhd->fcd/dot_general | solution.py:27
  54.5 14.9 %copy.74 = bf16[16,512,512]{2,0,1:T(8,128)(2,1)} copy(bf16[16,512,512]{1,2,0:T(8,128)(2,1)} %convert_bitcast_fusion.3) | data formatting | bytes 16777216 | tf_op jit(solution)/shard_map/optimization_barrier | solution.py:16
  69.4 7.9 all-to-all-start
  77.3 13.7 %fusion.16 = bf16[16,512,512]{2,1,0:T(8,128)(2,1)} fusion(bf16[16,512,512]{2,1,0:T(8,128)(2,1)} %param.10, bf16[1,16,512,512]{3,2,1,0:T(8,128)(2,1)} %param.6), kind=kOutput, calls=%fused_computation.32 | convolution fusion | flops 4299161600 | bytes 25165824 | tf_op jit(solution)/shard_map/acb,abd->acd/dot_general | solution.py:31
  91.0 136.4 %all-to-all-done = bf16[16,512,512]{2,0,1:T(8,128)(2,1)} async-done(((bf16[16,512,512]{2,0,1:T(8,128)(2,1)}), bf16[16,512,512]{2,0,1:T(8,128)(2,1)}, u32[]{:S(2)}, u32[]{:S(2)}) %all-to-all-start) | async-done | bytes 8388640 | tf_op jit(solution)/shard_map/all_to_all | solution.py:8
  227.4 12.3 %copy.76 = bf16[16,16,32,512]{3,2,1,0:T(8,128)(2,1)} copy(bf16[16,16,32,512]{3,1,2,0:T(8,128)(2,1)} %bitcast.6) | data formatting | bytes 16777216 | tf_op jit(solution)/shard_map/all_to_all | solution.py:8
  239.7 11.5 %copy.78 = bf16[16,512,512]{2,0,1:T(8,128)(2,1)} copy(bf16[16,512,512]{2,1,0:T(8,128)(2,1)} %fusion.16) | data formatting | bytes 16777216 | tf_op jit(solution)/shard_map/optimization_barrier | solution.py:16
  251.3 36.5 %all-to-all-start.1 = ((bf16[16,512,512]{2,0,1:T(8,128)(2,1)}), bf16[16,512,512]{2,0,1:T(8,128)(2,1)}, u32[]{:S(2)}, u32[]{:S(2)}) async-start(bf16[16,512,512]{2,0,1:T(8,128)(2,1)} %copy.78), calls=%async_computation.1 | async-start | bytes 16777216 | tf_op jit(solution)/shard_map/all_to_all | solution.py:8
  287.8 13.7 %copy.72 = bf16[256,32,512]{0,2,1:T(8,128)(2,1)} copy(bf16[256,32,512]{2,1,0:T(8,128)(2,1)} %param.8) | data formatting | bytes 16777216 | tf_op args[2]
  301.5 20.4 %convolution_bitcast_fusion.1 = f32[256,32,512]{0,2,1:T(8,128)} fusion(bf16[32,256,256]{2,1,0:T(8,128)(2,1)} %param.11, bf16[256,32,512]{2,1,0:T(8,128)(2,1)} %bitcast.90), kind=kOutput, calls=%fused_computation.17 | convolution fusion | flops 2147483648 | bytes 29360128 | tf_op jit(solution)/shard_map/cef,fcd->ecd/dot_general | solution.py:37
  321.9 14.5 %convert_bitcast_fusion.2 = bf16[256,32,512]{0,2,1:T(8,128)(2,1)} fusion(bf16[32,256,256]{2,1,0:T(8,128)(2,1)} %param.11, f32[256,32,512]{0,2,1:T(8,128)} %convolution_bitcast_fusion.1, bf16[256,32,512]{0,2,1:T(8,128)(2,1)} %copy.72), kind=kOutput, calls=%fused_computation.27 | convolution fusion | flops 2164260864 | bytes 37748736 | tf_op jit(solution)/shard_map/cea,ecd->acd/dot_general | solution.py:40
  336.4 102.0 %all-to-all-done.1 = bf16[16,512,512]{2,0,1:T(8,128)(2,1)} async-done(((bf16[16,512,512]{2,0,1:T(8,128)(2,1)}), bf16[16,512,512]{2,0,1:T(8,128)(2,1)}, u32[]{:S(2)}, u32[]{:S(2)}) %all-to-all-start.1) | async-done | bytes 8388640 | tf_op jit(solution)/shard_map/all_to_all | solution.py:8
  438.4 8.2 copy.79
  446.6 14.7 %copy.81 = bf16[256,32,512]{2,1,0:T(8,128)(2,1)} copy(bf16[256,32,512]{0,2,1:T(8,128)(2,1)} %convert_bitcast_fusion.2) | data formatting | bytes 16777216 | tf_op jit(solution)/shard_map/optimization_barrier | solution.py:16
  461.3 36.5 %all-to-all-start.2 = ((bf16[256,32,512]{2,1,0:T(8,128)(2,1)}), bf16[256,32,512]{2,1,0:T(8,128)(2,1)}, u32[]{:S(2)}, u32[]{:S(2)}) async-start(bf16[256,32,512]{2,1,0:T(8,128)(2,1)} %copy.81), calls=%async_computation.2 | async-start | bytes 16777216 | tf_op jit(solution)/shard_map/all_to_all | solution.py:12
  497.8 0.0 reduce-scatter.10.cloned.1.call-start
  497.9 12.8 %convolution_bitcast_fusion = f32[256,32,512]{0,2,1:T(8,128)} fusion(bf16[256,32,512]{2,0,1:T(8,128)(2,1)} %bitcast.88, bf16[32,256,256]{2,1,0:T(8,128)(2,1)} %param.11), kind=kOutput, calls=%fused_computation.16 | convolution fusion | flops 2147483648 | bytes 29360128 | tf_op jit(solution)/shard_map/cea,acd->ecd/dot_general | solution.py:45
  510.6 21.2 %fusion.14 = f32[32,256,256]{2,1,0:T(8,128)} fusion(bf16[256,32,512]{2,1,0:T(8,128)(2,1)} %bitcast.91, f32[256,32,512]{0,2,1:T(8,128)} %convolution_bitcast_fusion, bf16[256,32,512]{0,2,1:T(8,128)(2,1)} %copy.72), kind=kOutput, calls=%fused_computation.30 | convolution fusion | flops 2160066560 | bytes 41943040 | tf_op jit(solution)/shard_map/fcd,ecd->cef/dot_general | solution.py:55
  531.8 16.4 %multiply_convert_fusion.2 = bf16[32,256,256]{2,1,0:T(8,128)(2,1)} fusion(f32[32,256,256]{2,1,0:T(8,128)} %fusion.14, bf16[256,32,512]{2,0,1:T(8,128)(2,1)} %bitcast.89, f32[256,32,512]{0,2,1:T(8,128)} %convolution_bitcast_fusion.1, bf16[256,32,512]{0,2,1:T(8,128)(2,1)} %copy.72), kind=kOutput, calls=%fused_computation.24 | convolution fusion | flops 2166358016 | bytes 46137344 | tf_op jit(solution)/shard_map/ecd,acd->cea/dot_general | solution.py:56
  548.2 8.0 copy.102
  556.2 8.5 copy.104
  564.7 0.0 reduce-scatter.10.cloned.1.call-update
  564.7 14.6 %convert_bitcast_fusion.1 = bf16[256,32,512]{0,2,1:T(8,128)(2,1)} fusion(bf16[32,256,256]{2,1,0:T(8,128)(2,1)} %param.11, f32[256,32,512]{0,2,1:T(8,128)} %convolution_bitcast_fusion, bf16[256,32,512]{0,2,1:T(8,128)(2,1)} %copy.72), kind=kOutput, calls=%fused_computation.26 | convolution fusion | flops 2164260864 | bytes 37748736 | tf_op jit(solution)/shard_map/cef,ecd->fcd/dot_general | solution.py:47
  579.3 69.1 %all-to-all-done.2 = bf16[256,32,512]{2,1,0:T(8,128)(2,1)} async-done(((bf16[256,32,512]{2,1,0:T(8,128)(2,1)}), bf16[256,32,512]{2,1,0:T(8,128)(2,1)}, u32[]{:S(2)}, u32[]{:S(2)}) %all-to-all-start.2) | async-done | bytes 8388640 | tf_op jit(solution)/shard_map/all_to_all | solution.py:12
  648.4 8.3 copy.82
  656.7 14.7 %copy.83 = bf16[256,32,512]{2,1,0:T(8,128)(2,1)} copy(bf16[256,32,512]{0,2,1:T(8,128)(2,1)} %convert_bitcast_fusion.1) | data formatting | bytes 16777216 | tf_op jit(solution)/shard_map/optimization_barrier | solution.py:16
  671.3 36.5 %all-to-all-start.3 = ((bf16[256,32,512]{2,1,0:T(8,128)(2,1)}), bf16[256,32,512]{2,1,0:T(8,128)(2,1)}, u32[]{:S(2)}, u32[]{:S(2)}) async-start(bf16[256,32,512]{2,1,0:T(8,128)(2,1)} %copy.83), calls=%async_computation.3 | async-start | bytes 16777216 | tf_op jit(solution)/shard_map/all_to_all | solution.py:12
  707.9 0.0 reduce-scatter.6.cloned.1.call-start
  707.9 14.9 %multiply_convert_fusion.1 = bf16[256,32,512]{0,2,1:T(8,128)(2,1)} fusion(f32[256,32,512]{0,2,1:T(8,128)} %convolution_bitcast_fusion.1, f32[256,32,512]{0,2,1:T(8,128)} %convolution_bitcast_fusion), kind=kLoop, calls=%fused_computation.14 | loop fusion | flops 8388608 | bytes 41943040 | tf_op jit(solution)/shard_map/convert_element_type | solution.py:52
  722.9 0.0 reduce-scatter.6.cloned.1.call-update
  722.9 0.0 reduce-scatter.8.cloned.1.call-start
  722.9 16.1 %fusion.9 = f32[16,512,512]{2,1,0:T(8,128)} fusion(bf16[16,512,512]{2,1,0:T(8,128)(2,1)} %bitcast.92, bf16[1,16,512,512]{3,2,1,0:T(8,128)(2,1)} %param.6), kind=kOutput, calls=%fused_computation.20 | convolution fusion | flops 4294967296 | bytes 33554432 | tf_op jit(solution)/shard_map/acd,abd->acb/dot_general | solution.py:65
  739.0 119.5 %all-to-all-done.3 = bf16[256,32,512]{2,1,0:T(8,128)(2,1)} async-done(((bf16[256,32,512]{2,1,0:T(8,128)(2,1)}), bf16[256,32,512]{2,1,0:T(8,128)(2,1)}, u32[]{:S(2)}, u32[]{:S(2)}) %all-to-all-start.3) | async-done | bytes 8388640 | tf_op jit(solution)/shard_map/all_to_all | solution.py:12
  858.5 8.3 copy.84
  866.7 15.7 %multiply_convert_fusion = bf16[16,512,512]{2,1,0:T(8,128)(2,1)} fusion(f32[16,512,512]{2,1,0:T(8,128)} %fusion.9, bf16[16,512,512]{2,1,0:T(8,128)(2,1)} %bitcast.94, bf16[16,512,512]{1,2,0:T(8,128)(2,1)} %fusion.2), kind=kOutput, calls=%fused_computation.13 | convolution fusion | flops 4307550208 | bytes 41943040 | tf_op jit(solution)/shard_map/fhd,fcd->fch/dot_general | solution.py:72
  882.4 0.0 reduce-scatter.8.cloned.1.call-update
  882.5 0.0 reduce-scatter.10.cloned.1.call-done
  882.5 2.2 copy.105
  884.7 3.0 copy.103
  887.7 11.4 %convert_bitcast_fusion = bf16[1,16,512,512]{2,3,1,0:T(8,128)(2,1)} fusion(bf16[16,512,512]{2,1,0:T(8,128)(2,1)} %bitcast.93, bf16[16,512,512]{2,1,0:T(8,128)(2,1)} %param.10), kind=kOutput, calls=%fused_computation.25 | convolution fusion | flops 4299161600 | bytes 25165824 | tf_op jit(solution)/shard_map/acb,acd->abd/dot_general | solution.py:62
  899.1 12.3 %copy.92 = bf16[1,16,512,512]{3,2,1,0:T(8,128)(2,1)} copy(bf16[1,16,512,512]{2,3,1,0:T(8,128)(2,1)} %convert_bitcast_fusion) | data formatting | bytes 16777216
  911.4 0.0 reduce-scatter.6.cloned.1.call-done
  911.4 7.8 copy.94
  919.2 21.2 %fusion.8 = (bf16[1,16,512,512]{2,3,1,0:T(8,128)(2,1)}, bf16[1,16,512,512]{2,3,1,0:T(8,128)(2,1)}) fusion(bf16[1,16,512,512]{2,3,1,0:T(8,128)(2,1)} %copy.73, bf16[1,16,512,512]{2,3,1,0:T(8,128)(2,1)} %copy.71, bf16[16,512,512]{2,1,0:T(8,128)(2,1)} %bitcast.95, bf16[16,512,512]{2,1,0:T(8,128)(2,1)} %param.10), kind=kOutput, calls=%fused_computation.19 | convolution fusion | flops 4353687552 | bytes 50331648 | tf_op jit(solution)/shard_map/fch,fcd->fhd/dot_general | solution.py:66
  940.4 12.4 %copy.93 = bf16[1,16,512,512]{3,2,1,0:T(8,128)(2,1)} copy(bf16[1,16,512,512]{2,3,1,0:T(8,128)(2,1)} %get-tuple-element.42) | data formatting | bytes 16777216
  952.8 12.3 %copy.91 = bf16[1,16,512,512]{3,2,1,0:T(8,128)(2,1)} copy(bf16[1,16,512,512]{2,3,1,0:T(8,128)(2,1)} %get-tuple-element.43) | data formatting | bytes 16777216
  965.1 48.7 %reduce-scatter.8.cloned.1.call-done = bf16[16,512,256]{2,1,0:T(8,128)(2,1)} async-done(((bf16[16,512,512]{2,1,0:T(8,128)(2,1)}), bf16[16,512,256]{2,1,0:T(8,128)(2,1)}) %reduce-scatter.8.cloned.1.call-update) | async-done | bytes 4194320 | tf_op jit(solution)/shard_map/reduce_scatter | solution.py:74
Async XLA Ops:
  69.4 158.0 %all-to-all-start = ((bf16[16,512,512]{2,0,1:T(8,128)(2,1)}), bf16[16,512,512]{2,0,1:T(8,128)(2,1)}, u32[]{:S(2)}, u32[]{:S(2)}) async-start(bf16[16,512,512]{2,0,1:T(8,128)(2,1)} %copy.74), calls=%async_computation | async-start | bytes 16777216 | tf_op jit(solution)/shard_map/all_to_all | solution.py:8
  251.3 187.1 %all-to-all-start.1 = ((bf16[16,512,512]{2,0,1:T(8,128)(2,1)}), bf16[16,512,512]{2,0,1:T(8,128)(2,1)}, u32[]{:S(2)}, u32[]{:S(2)}) async-start(bf16[16,512,512]{2,0,1:T(8,128)(2,1)} %copy.78), calls=%async_computation.1 | async-start | bytes 16777216 | tf_op jit(solution)/shard_map/all_to_all | solution.py:8
  461.3 187.1 %all-to-all-start.2 = ((bf16[256,32,512]{2,1,0:T(8,128)(2,1)}), bf16[256,32,512]{2,1,0:T(8,128)(2,1)}, u32[]{:S(2)}, u32[]{:S(2)}) async-start(bf16[256,32,512]{2,1,0:T(8,128)(2,1)} %copy.81), calls=%async_computation.2 | async-start | bytes 16777216 | tf_op jit(solution)/shard_map/all_to_all | solution.py:12
  497.8 384.7 %reduce-scatter.10.cloned.1.call-start = ((), (), s32[]{:S(2)}) async-start(), calls=%async_computation.9 | async-start | bytes 6291456
  671.3 187.1 %all-to-all-start.3 = ((bf16[256,32,512]{2,1,0:T(8,128)(2,1)}), bf16[256,32,512]{2,1,0:T(8,128)(2,1)}, u32[]{:S(2)}, u32[]{:S(2)}) async-start(bf16[256,32,512]{2,1,0:T(8,128)(2,1)} %copy.83), calls=%async_computation.3 | async-start | bytes 16777216 | tf_op jit(solution)/shard_map/all_to_all | solution.py:12
  707.9 203.5 %reduce-scatter.6.cloned.1.call-start = ((), (), s32[]{:S(2)}) async-start(), calls=%async_computation.7 | async-start | bytes 12582912 | tf_op jit(solution)/shard_map/reduce_scatter | solution.py:60
  722.9 290.9 %reduce-scatter.8.cloned.1.call-start = ((), (), s32[]{:S(2)}) async-start(), calls=%async_computation.8 | async-start | bytes 12582912 | tf_op jit(solution)/shard_map/reduce_scatter | solution.py:74
Sparse Core Ops, SparseCore 0:
  564.9 55.6 reduce-scatter.9
  723.0 100.6 reduce-scatter.5
  882.6 131.1 reduce-scatter.7
where the time goes:
time: 1030 us; the launch traced here: 1020 us
  waiting for transfers between devices  476 us (46%)
  local copies, waits for them, and re-layouts  198 us (19%)
  matrix products  189 us (18%)
  starting transfers between devices  118 us (11%)
  other arithmetic  26.3 us (3%)
  between operations  14 us (1%)
    all_to_all x2, waiting for transfers between devices, to_cols(): return lax.all_to_all(x, 'seq', split_axis=1, concat_axis=0, tiled=True)  238 us
    all_to_all x2, waiting for transfers between devices, to_rows(): return lax.all_to_all(x, 'seq', split_axis=0, concat_axis=1, tiled=True)  189 us
    unnamed x11, local copies, waits for them, and re-layouts  105 us
    all_to_all x2, starting transfers between devices, to_rows(): return lax.all_to_all(x, 'seq', split_axis=0, concat_axis=1, tiled=True)  73.1 us
    optimization_barrier x4, local copies, waits for them, and re-layouts, held(): return lax.optimization_barrier(x)  55.8 us
    reduce_scatter x1, waiting for transfers between devices, body(): lax.psum_scatter(grad_block_one, 'dp', scatter_dimension=2, tiled=True)  48.7 us
    all_to_all x2, starting transfers between devices, to_cols(): return lax.all_to_all(x, 'seq', split_axis=1, concat_axis=0, tiled=True)  44.4 us
    dot_general x1, matrix products, body(): jnp.einsum('fch,fcd->fhd', block_one, third_rows, preferred_element_type=...  21.2 us
  transfers between devices with their start and end apart: 7, of which 5 were waited for; matrix products, arithmetic and copies ran while one was open for 30% of the time, Pallas kernels for 0%

commit v1 on v0

--- a/solution.py
+++ b/solution.py
@@ -5,7 +5,16 @@
 
 
 def to_cols(x):
-    return lax.all_to_all(x, "seq", split_axis=1, concat_axis=0, tiled=True)
+    _touch_forms = lambda x0, ax_name: jnp.concatenate(
+        jax.lax.all_to_all(
+            jnp.stack(jnp.split(x0, jax.lax.axis_size(ax_name), axis=1), axis=0),
+            axis_name=ax_name,
+            split_axis=0,
+            concat_axis=0,
+        ),
+        axis=0,
+    )
+    return _touch_forms(x, "seq")
 
 
 def to_rows(x):

time: 1030 us -> 1090 us (1.058)
  local copies, waits for them, and re-layouts: 198 us -> 256 us
  matrix products: 189 us -> 203 us
  waiting for transfers between devices: 476 us -> 463 us
    another operation x0 -> x19, local copies, waits for them, and re-layouts: none -> 62.5 us  [to_cols(): jnp.stack(jnp.split(x0, jax.lax.axis_size(ax_name), axis=1), axis=0)]
    unnamed x11 -> x55, local copies, waits for them, and re-layouts: 105 us -> 148 us
    optimization_barrier x4 -> x2, local copies, waits for them, and re-layouts: 55.8 us -> 29.2 us  [held(): return lax.optimization_barrier(x)]
    all_to_all x2 -> x0, local copies, waits for them, and re-layouts: 20.5 us -> none  [to_cols(): return lax.all_to_all(x, 'seq', split_axis=1, concat_axis=0, tiled=True)]
    all_to_all x2, waiting for transfers between devices: 189 us -> 175 us  [to_rows(): return lax.all_to_all(x, 'seq', split_axis=0, concat_axis=1, tiled=True)]
  transfers between devices with their start and end apart: 7 -> 7, of which waited for: 5 -> 5; matrix products, arithmetic and copies ran while one was open for 30% -> 29% of each run, Pallas kernels for 0% -> 0%
where the time goes in v1:
time: 1090 us; the launch traced here: 1080 us
  waiting for transfers between devices  463 us (42%)
  local copies, waits for them, and re-layouts  256 us (23%)
  matrix products  203 us (19%)
  starting transfers between devices  117 us (11%)
  other arithmetic  26.3 us (2%)
  between operations  14.3 us (1%)
    all_to_all x2, waiting for transfers between devices, to_cols(): jax.lax.all_to_all(jnp.stack(jnp.split(x0, jax.lax.axis_size(ax_name), ax...  239 us
    all_to_all x2, waiting for transfers between devices, to_rows(): return lax.all_to_all(x, 'seq', split_axis=0, concat_axis=1, tiled=True)  175 us
    unnamed x55, local copies, waits for them, and re-layouts  148 us
    all_to_all x2, starting transfers between devices, to_rows(): return lax.all_to_all(x, 'seq', split_axis=0, concat_axis=1, tiled=True)  73.1 us
    another operation x19, local copies, waits for them, and re-layouts, to_cols(): jnp.stack(jnp.split(x0, jax.lax.axis_size(ax_name), axis=1), axis=0)  62.5 us
    reduce_scatter x1, waiting for transfers between devices, body(): lax.psum_scatter(grad_block_one, 'dp', scatter_dimension=2, tiled=True)  48.7 us
    all_to_all x2, starting transfers between devices, to_cols(): jax.lax.all_to_all(jnp.stack(jnp.split(x0, jax.lax.axis_size(ax_name), ax...  44.2 us
    optimization_barrier x2, local copies, waits for them, and re-layouts, held(): return lax.optimization_barrier(x)  29.2 us
  transfers between devices with their start and end apart: 7, of which 5 were waited for; matrix products, arithmetic and copies ran while one was open for 29% of the time, Pallas kernels for 0%

profile of v1, /device:TPU:0, one launch (start us, length us, event | category | flops | bytes accessed | tf_op | source)
XLA Modules:
  0.0 1079.6 jit_solution(10921028470349587351)
XLA Ops:
  7.2 12.3 %copy.69 = bf16[1,16,512,512]{2,3,1,0:T(8,128)(2,1)} copy(bf16[1,16,512,512]{3,2,1,0:T(8,128)(2,1)} %param.7) | data formatting | bytes 16777216 | tf_op args[1]
  19.4 12.3 %copy.71 = bf16[1,16,512,512]{2,3,1,0:T(8,128)(2,1)} copy(bf16[1,16,512,512]{3,2,1,0:T(8,128)(2,1)} %param.9) | data formatting | bytes 16777216 | tf_op args[3]
  31.7 11.4 %fusion.2 = bf16[16,512,512]{1,2,0:T(8,128)(2,1)} fusion(bf16[1,16,512,512]{2,3,1,0:T(8,128)(2,1)} %copy.71, bf16[1,16,512,512]{2,3,1,0:T(8,128)(2,1)} %copy.69), kind=kLoop, calls=%fused_computation.6 | loop fusion | flops 29360128 | bytes 25165824 | tf_op jit(solution)/shard_map/convert_element_type | solution.py:35
  43.1 11.5 %convert_bitcast_fusion.3 = bf16[16,512,512]{1,2,0:T(8,128)(2,1)} fusion(bf16[16,512,512]{1,2,0:T(8,128)(2,1)} %fusion.2, bf16[16,512,512]{2,1,0:T(8,128)(2,1)} %param.10), kind=kOutput, calls=%fused_computation.28 | convolution fusion | flops 4299161600 | bytes 25165824 | tf_op jit(solution)/shard_map/fch,fhd->fcd/dot_general | solution.py:36
  54.5 22.1 %slice_bitcast_fusion = (bf16[1,16,32,512]{2,3,1,0:T(8,128)(2,1)}, bf16[1,16,32,512]{2,3,1,0:T(8,128)(2,1)}, bf16[1,16,32,512]{2,3,1,0:T(8,128)(2,1)}, bf16[1,16...) fusion(bf16[16,512,512]{1,2,0:T(8,128)(2,1)} %convert_bitcast_f, ...), kind=kLoop, calls=%fused_computation.37 | loop fusion | bytes 16777216 | tf_op jit(solution)/shard_map/stack | solution.py:10
  80.4 2.6 copy.85
  83.0 2.6 copy.84
  85.5 2.6 copy.83
  88.1 2.6 copy.82
  90.7 2.6 copy.81
  93.2 2.6 copy.80
  95.8 2.6 copy.79
  98.4 2.6 copy.78
  101.0 2.6 copy.77
  103.6 2.6 copy.76
  106.2 2.6 copy.75
  108.7 2.6 copy.74
  111.3 2.6 copy.73
  115.4 2.0 constant_dynamic-update-slice_fusion.15
  117.4 1.9 constant_dynamic-update-slice_fusion.14
  119.3 1.9 constant_dynamic-update-slice_fusion.13
  121.2 1.9 constant_dynamic-update-slice_fusion.12
  123.1 1.9 constant_dynamic-update-slice_fusion.11
  125.0 1.9 constant_dynamic-update-slice_fusion.10
  128.8 1.9 constant_dynamic-update-slice_fusion.8
  137.5 7.6 all-to-all-start
  145.1 13.7 %fusion.19 = bf16[16,512,512]{2,1,0:T(8,128)(2,1)} fusion(bf16[16,512,512]{2,1,0:T(8,128)(2,1)} %param.10, bf16[1,16,512,512]{3,2,1,0:T(8,128)(2,1)} %param.6), kind=kOutput, calls=%fused_computation.35 | convolution fusion | flops 4299161600 | bytes 25165824 | tf_op jit(solution)/shard_map/acb,abd->acd/dot_general | solution.py:40
  158.8 136.9 %all-to-all-done = bf16[16,16,32,512]{3,2,1,0:T(8,128)(2,1)} async-done(((bf16[16,16,32,512]{3,2,1,0:T(8,128)(2,1)}), bf16[16,16,32,512]{3,2,1,0:T(8,128)(2,1)}, u32[]{:S(2)}, u32[]{:S(2)}) %all-to-all-start) | async-done | bytes 8388640 | tf_op jit(solution)/shard_map/all_to_all | solution.py:9
  295.7 2.0 bitcast_dynamic-update-slice_fusion.15
  297.7 2.6 bitcast_dynamic-update-slice_fusion.14
  300.3 1.9 bitcast_dynamic-update-slice_fusion.13
  302.2 1.9 bitcast_dynamic-update-slice_fusion.12
  307.9 1.9 bitcast_dynamic-update-slice_fusion.9
  318.5 36.5 %all-to-all-start.1 = ((bf16[16,16,32,512]{3,2,1,0:T(8,128)(2,1)}), bf16[16,16,32,512]{3,2,1,0:T(8,128)(2,1)}, u32[]{:S(2)}, u32[]{:S(2)}) async-start(bf16[16,16,32,512]{3,2,1,0:T(8,128)(2,1)} %bitcast_dynamic-update-slice_fusion), calls=%async_computation.1 | async-start | bytes 16777216 | tf_op jit(solution)/shard_map/all_to_all | solution.py:9
  355.0 13.7 %copy.70 = bf16[256,32,512]{0,2,1:T(8,128)(2,1)} copy(bf16[256,32,512]{2,1,0:T(8,128)(2,1)} %param.8) | data formatting | bytes 16777216 | tf_op args[2]
  368.7 20.4 %convolution_bitcast_fusion.1 = f32[256,32,512]{0,2,1:T(8,128)} fusion(bf16[32,256,256]{2,1,0:T(8,128)(2,1)} %param.11, bf16[256,32,512]{2,1,0:T(8,128)(2,1)} %bitcast.20), kind=kOutput, calls=%fused_computation.17 | convolution fusion | flops 2147483648 | bytes 29360128 | tf_op jit(solution)/shard_map/cef,fcd->ecd/dot_general | solution.py:46
  389.1 14.5 %convert_bitcast_fusion.2 = bf16[256,32,512]{0,2,1:T(8,128)(2,1)} fusion(bf16[32,256,256]{2,1,0:T(8,128)(2,1)} %param.11, f32[256,32,512]{0,2,1:T(8,128)} %convolution_bitcast_fusion.1, bf16[256,32,512]{0,2,1:T(8,128)(2,1)} %copy.70), kind=kOutput, calls=%fused_computation.27 | convolution fusion | flops 2164260864 | bytes 37748736 | tf_op jit(solution)/shard_map/cea,ecd->acd/dot_general | solution.py:49
  403.6 102.0 %all-to-all-done.1 = bf16[16,16,32,512]{3,2,1,0:T(8,128)(2,1)} async-done(((bf16[16,16,32,512]{3,2,1,0:T(8,128)(2,1)}), bf16[16,16,32,512]{3,2,1,0:T(8,128)(2,1)}, u32[]{:S(2)}, u32[]{:S(2)}) %all-to-all-start.1) | async-done | bytes 8388640 | tf_op jit(solution)/shard_map/all_to_all | solution.py:9
  505.6 14.6 %copy.90 = bf16[256,32,512]{2,1,0:T(8,128)(2,1)} copy(bf16[256,32,512]{0,2,1:T(8,128)(2,1)} %convert_bitcast_fusion.2) | data formatting | bytes 16777216 | tf_op jit(solution)/shard_map/optimization_barrier | solution.py:25
  520.2 36.5 %all-to-all-start.2 = ((bf16[256,32,512]{2,1,0:T(8,128)(2,1)}), bf16[256,32,512]{2,1,0:T(8,128)(2,1)}, u32[]{:S(2)}, u32[]{:S(2)}) async-start(bf16[256,32,512]{2,1,0:T(8,128)(2,1)} %copy.90), calls=%async_computation.2 | async-start | bytes 16777216 | tf_op jit(solution)/shard_map/all_to_all | solution.py:21
  556.8 20.4 %convolution_bitcast_fusion = f32[256,32,512]{0,2,1:T(8,128)} fusion(bf16[32,256,256]{2,1,0:T(8,128)(2,1)} %param.11, bf16[256,32,512]{2,1,0:T(8,128)(2,1)} %bitcast.39), kind=kOutput, calls=%fused_computation.16 | convolution fusion | flops 2147483648 | bytes 29360128 | tf_op jit(solution)/shard_map/cea,acd->ecd/dot_general | solution.py:54
  577.2 21.3 %fusion.14 = f32[32,256,256]{2,1,0:T(8,128)} fusion(bf16[256,32,512]{2,1,0:T(8,128)(2,1)} %bitcast.39, f32[256,32,512]{0,2,1:T(8,128)} %convolution_bitcast_fusion.1, bf16[256,32,512]{0,2,1:T(8,128)(2,1)} %copy.70), kind=kOutput, calls=%fused_computation.30 | convolution fusion | flops 2160066560 | bytes 41943040 | tf_op jit(solution)/shard_map/ecd,acd->cea/dot_general | solution.py:65
  598.5 22.0 %multiply_convert_fusion.2 = bf16[32,256,256]{2,1,0:T(8,128)(2,1)} fusion(f32[32,256,256]{2,1,0:T(8,128)} %fusion.14, bf16[256,32,512]{2,1,0:T(8,128)(2,1)} %bitcast.20, f32[256,32,512]{0,2,1:T(8,128)} %convolution_bitcast_fusion, bf16[256,32,512]{0,2,1:T(8,128)(2,1)} %copy.70), kind=kOutput, calls=%fused_computation.24 | convolution fusion | flops 2166358016 | bytes 46137344 | tf_op jit(solution)/shard_map/fcd,ecd->cef/dot_general | solution.py:64
  620.6 8.0 copy.110
  628.6 8.5 copy.112
  637.1 14.5 %convert_bitcast_fusion.1 = bf16[256,32,512]{0,2,1:T(8,128)(2,1)} fusion(bf16[32,256,256]{2,1,0:T(8,128)(2,1)} %param.11, f32[256,32,512]{0,2,1:T(8,128)} %convolution_bitcast_fusion, bf16[256,32,512]{0,2,1:T(8,128)(2,1)} %copy.70), kind=kOutput, calls=%fused_computation.26 | convolution fusion | flops 2164260864 | bytes 37748736 | tf_op jit(solution)/shard_map/cef,ecd->fcd/dot_general | solution.py:56
  651.6 55.8 %all-to-all-done.2 = bf16[256,32,512]{2,1,0:T(8,128)(2,1)} async-done(((bf16[256,32,512]{2,1,0:T(8,128)(2,1)}), bf16[256,32,512]{2,1,0:T(8,128)(2,1)}, u32[]{:S(2)}, u32[]{:S(2)}) %all-to-all-start.2) | async-done | bytes 8388640 | tf_op jit(solution)/shard_map/all_to_all | solution.py:21
  707.3 8.3 copy.91
  715.6 14.5 %copy.92 = bf16[256,32,512]{2,1,0:T(8,128)(2,1)} copy(bf16[256,32,512]{0,2,1:T(8,128)(2,1)} %convert_bitcast_fusion.1) | data formatting | bytes 16777216 | tf_op jit(solution)/shard_map/optimization_barrier | solution.py:25
  730.1 36.5 %all-to-all-start.3 = ((bf16[256,32,512]{2,1,0:T(8,128)(2,1)}), bf16[256,32,512]{2,1,0:T(8,128)(2,1)}, u32[]{:S(2)}, u32[]{:S(2)}) async-start(bf16[256,32,512]{2,1,0:T(8,128)(2,1)} %copy.92), calls=%async_computation.3 | async-start | bytes 16777216 | tf_op jit(solution)/shard_map/all_to_all | solution.py:21
  766.7 14.9 %multiply_convert_fusion.1 = bf16[256,32,512]{0,2,1:T(8,128)(2,1)} fusion(f32[256,32,512]{0,2,1:T(8,128)} %convolution_bitcast_fusion.1, f32[256,32,512]{0,2,1:T(8,128)} %convolution_bitcast_fusion), kind=kLoop, calls=%fused_computation.14 | loop fusion | flops 8388608 | bytes 41943040 | tf_op jit(solution)/shard_map/convert_element_type | solution.py:61
  781.8 16.1 %fusion.9 = f32[16,512,512]{2,1,0:T(8,128)} fusion(bf16[16,512,512]{2,1,0:T(8,128)(2,1)} %bitcast.144, bf16[1,16,512,512]{3,2,1,0:T(8,128)(2,1)} %param.6), kind=kOutput, calls=%fused_computation.20 | convolution fusion | flops 4294967296 | bytes 33554432 | tf_op jit(solution)/shard_map/acd,abd->acb/dot_general | solution.py:74
  797.8 119.4 %all-to-all-done.3 = bf16[256,32,512]{2,1,0:T(8,128)(2,1)} async-done(((bf16[256,32,512]{2,1,0:T(8,128)(2,1)}), bf16[256,32,512]{2,1,0:T(8,128)(2,1)}, u32[]{:S(2)}, u32[]{:S(2)}) %all-to-all-start.3) | async-done | bytes 8388640 | tf_op jit(solution)/shard_map/all_to_all | solution.py:21
  917.3 8.3 copy.93
  925.5 15.7 %multiply_convert_fusion = bf16[16,512,512]{2,1,0:T(8,128)(2,1)} fusion(f32[16,512,512]{2,1,0:T(8,128)} %fusion.9, bf16[16,512,512]{2,1,0:T(8,128)(2,1)} %bitcast.146, bf16[16,512,512]{1,2,0:T(8,128)(2,1)} %fusion.2), kind=kOutput, calls=%fused_computation.13 | convolution fusion | flops 4307550208 | bytes 41943040 | tf_op jit(solution)/shard_map/fhd,fcd->fch/dot_general | solution.py:81
  941.3 2.2 copy.113
  943.5 3.0 copy.111
  946.6 11.4 %convert_bitcast_fusion = bf16[1,16,512,512]{2,3,1,0:T(8,128)(2,1)} fusion(bf16[16,512,512]{2,1,0:T(8,128)(2,1)} %bitcast.145, bf16[16,512,512]{2,1,0:T(8,128)(2,1)} %param.10), kind=kOutput, calls=%fused_computation.25 | convolution fusion | flops 4299161600 | bytes 25165824 | tf_op jit(solution)/shard_map/acb,acd->abd/dot_general | solution.py:71
  957.9 12.3 %copy.102 = bf16[1,16,512,512]{3,2,1,0:T(8,128)(2,1)} copy(bf16[1,16,512,512]{2,3,1,0:T(8,128)(2,1)} %convert_bitcast_fusion) | data formatting | bytes 16777216
  970.2 7.8 copy.104
  978.0 21.2 %fusion.8 = (bf16[1,16,512,512]{2,3,1,0:T(8,128)(2,1)}, bf16[1,16,512,512]{2,3,1,0:T(8,128)(2,1)}) fusion(bf16[1,16,512,512]{2,3,1,0:T(8,128)(2,1)} %copy.71, bf16[1,16,512,512]{2,3,1,0:T(8,128)(2,1)} %copy.69, bf16[16,512,512]{2,1,0:T(8,128)(2,1)} %bitcast.147, bf16[16,512,512]{2,1,0:T(8,128)(2,1)} %param.10), kind=kOutput, calls=%fused_computation.19 | convolution fusion | flops 4353687552 | bytes 50331648 | tf_op jit(solution)/shard_map/fch,fcd->fhd/dot_general | solution.py:75
  999.2 12.4 %copy.103 = bf16[1,16,512,512]{3,2,1,0:T(8,128)(2,1)} copy(bf16[1,16,512,512]{2,3,1,0:T(8,128)(2,1)} %get-tuple-element.42) | data formatting | bytes 16777216
  1011.6 12.3 %copy.101 = bf16[1,16,512,512]{3,2,1,0:T(8,128)(2,1)} copy(bf16[1,16,512,512]{2,3,1,0:T(8,128)(2,1)} %get-tuple-element.43) | data formatting | bytes 16777216
  1023.9 48.7 %reduce-scatter.8.cloned.1.call-done = bf16[16,512,256]{2,1,0:T(8,128)(2,1)} async-done(((bf16[16,512,512]{2,1,0:T(8,128)(2,1)}), bf16[16,512,256]{2,1,0:T(8,128)(2,1)}) %reduce-scatter.8.cloned.1.call-update) | async-done | bytes 4194320 | tf_op jit(solution)/shard_map/reduce_scatter | solution.py:83
  (45 shorter events, 26.5 us)
Async XLA Ops:
  115.4 15.3 %copy-start.6 = (bf16[1,16,32,512]{3,2,1,0:T(8,128)(2,1)S(1)}, bf16[1,16,32,512]{3,2,1,0:T(8,128)(2,1)}, u32[]{:S(2)}) copy-start(bf16[1,16,32,512]{3,2,1,0:T(8,128)(2,1)} %copy.80) | copy-start | bytes 1572868
  115.4 16.2 %copy-start.5 = (bf16[1,16,32,512]{3,2,1,0:T(8,128)(2,1)S(1)}, bf16[1,16,32,512]{3,2,1,0:T(8,128)(2,1)}, u32[]{:S(2)}) copy-start(bf16[1,16,32,512]{3,2,1,0:T(8,128)(2,1)} %copy.81) | copy-start | bytes 1572868
  115.4 17.0 %copy-start.4 = (bf16[1,16,32,512]{3,2,1,0:T(8,128)(2,1)S(1)}, bf16[1,16,32,512]{3,2,1,0:T(8,128)(2,1)}, u32[]{:S(2)}) copy-start(bf16[1,16,32,512]{3,2,1,0:T(8,128)(2,1)} %copy.82) | copy-start | bytes 1572868
  115.4 17.9 %copy-start.3 = (bf16[1,16,32,512]{3,2,1,0:T(8,128)(2,1)S(1)}, bf16[1,16,32,512]{3,2,1,0:T(8,128)(2,1)}, u32[]{:S(2)}) copy-start(bf16[1,16,32,512]{3,2,1,0:T(8,128)(2,1)} %copy.83) | copy-start | bytes 1572868
  115.4 18.7 %copy-start.2 = (bf16[1,16,32,512]{3,2,1,0:T(8,128)(2,1)S(1)}, bf16[1,16,32,512]{3,2,1,0:T(8,128)(2,1)}, u32[]{:S(2)}) copy-start(bf16[1,16,32,512]{3,2,1,0:T(8,128)(2,1)} %copy.84) | copy-start | bytes 1572868
  115.4 19.6 %copy-start.1 = (bf16[1,16,32,512]{3,2,1,0:T(8,128)(2,1)S(1)}, bf16[1,16,32,512]{3,2,1,0:T(8,128)(2,1)}, u32[]{:S(2)}) copy-start(bf16[1,16,32,512]{3,2,1,0:T(8,128)(2,1)} %copy.85) | copy-start | bytes 1572868
  137.5 158.2 %all-to-all-start = ((bf16[16,16,32,512]{3,2,1,0:T(8,128)(2,1)}), bf16[16,16,32,512]{3,2,1,0:T(8,128)(2,1)}, u32[]{:S(2)}, u32[]{:S(2)}) async-start(bf16[16,16,32,512]{3,2,1,0:T(8,128)(2,1)} %constant_dynamic-update-slice_fusion), calls=%async_computation | async-start | bytes 16777216 | tf_op jit(solution)/shard_map/all_to_all | solution.py:9
  295.7 16.0 %copy-start = (bf16[16,512,512]{2,1,0:T(8,128)(2,1)S(1)}, bf16[16,512,512]{2,1,0:T(8,128)(2,1)}, u32[]{:S(2)}) copy-start(bf16[16,512,512]{2,1,0:T(8,128)(2,1)} %fusion.19) | copy-start | bytes 25165828
  318.5 187.1 %all-to-all-start.1 = ((bf16[16,16,32,512]{3,2,1,0:T(8,128)(2,1)}), bf16[16,16,32,512]{3,2,1,0:T(8,128)(2,1)}, u32[]{:S(2)}, u32[]{:S(2)}) async-start(bf16[16,16,32,512]{3,2,1,0:T(8,128)(2,1)} %bitcast_dynamic-update-slice_fusion), calls=%async_computation.1 | async-start | bytes 16777216 | tf_op jit(solution)/shard_map/all_to_all | solution.py:9
  520.2 187.1 %all-to-all-start.2 = ((bf16[256,32,512]{2,1,0:T(8,128)(2,1)}), bf16[256,32,512]{2,1,0:T(8,128)(2,1)}, u32[]{:S(2)}, u32[]{:S(2)}) async-start(bf16[256,32,512]{2,1,0:T(8,128)(2,1)} %copy.90), calls=%async_computation.2 | async-start | bytes 16777216 | tf_op jit(solution)/shard_map/all_to_all | solution.py:21
  556.8 384.6 %reduce-scatter.10.cloned.1.call-start = ((), (), s32[]{:S(2)}) async-start(), calls=%async_computation.9 | async-start | bytes 6291456
  730.1 187.1 %all-to-all-start.3 = ((bf16[256,32,512]{2,1,0:T(8,128)(2,1)}), bf16[256,32,512]{2,1,0:T(8,128)(2,1)}, u32[]{:S(2)}, u32[]{:S(2)}) async-start(bf16[256,32,512]{2,1,0:T(8,128)(2,1)} %copy.92), calls=%async_computation.3 | async-start | bytes 16777216 | tf_op jit(solution)/shard_map/all_to_all | solution.py:21
  766.7 203.5 %reduce-scatter.6.cloned.1.call-start = ((), (), s32[]{:S(2)}) async-start(), calls=%async_computation.7 | async-start | bytes 12582912 | tf_op jit(solution)/shard_map/reduce_scatter | solution.py:69
  781.7 290.9 %reduce-scatter.8.cloned.1.call-start = ((), (), s32[]{:S(2)}) async-start(), calls=%async_computation.8 | async-start | bytes 12582912 | tf_op jit(solution)/shard_map/reduce_scatter | solution.py:83
Sparse Core Ops, SparseCore 0:
  637.2 55.6 reduce-scatter.9
  781.8 100.6 reduce-scatter.5
  941.4 131.1 reduce-scatter.7
